TPU v7x, 512 devices: a whole 4x8x8 slice. The times are simulated.
512 devices in a mesh: pairs: 64 (over x, y, core), aux: 8 (over z).
Axes of the slice: x: 4, y: 8, z: 8, core: 2. Of those that a mesh axis runs over, the one named last changes fastest.
Arguments:
- amplitudes: bfloat16 [1024, 128, 128], P('pairs'), may hold values from -6 to 6
- pno_coef: bfloat16 [1024, 256, 128], P('pairs'), may hold values from -0.625 to 0.625
- ladder_ints: bfloat16 [320, 128, 128], P('aux'), may hold values from -0.3125 to 0.3125
- coulomb_ints: bfloat16 [1024, 128, 128], P(('pairs', 'aux')), may hold values from -6 to 6
- pno_energy: float32 [1024, 128], P(('pairs', 'aux')), may hold values from 0.3 to 3
- link_owner: int32 [49152, 1], P(('pairs', 'aux')), may hold values from 0 to 63; in each aligned block of 96 rows (0 to 95, 96 to 191, ...) at most 2 rows name the same one
- link_local: int32 [49152, 1], P(('pairs', 'aux')), may hold values from 0 to 15
Outputs:
- updated: float32 [1024, 128, 128], P(('pairs', 'aux'))
Inputs may be any that keep to these rules, and one draw needn't show every extreme that they name: `link_owner`: in each device's aligned block of 96 rows no owner group is named by more than 2 rows, a bound that some block reaches.
All inputs are finite; a program needn't handle non-finite values.
Results may differ from a plain program's by a relative error of at most 0.0033.
Values may be sent and summed in bfloat16 or wider, within the bound.
No kernel may reach another device: no remote copies, remote signals or barrier semaphores. Data moves between devices by JAX's collectives and lax.ppermute only.
A program may use at most 128 MiB of HBM per device.

v0:
```python
import jax
import jax.numpy as jnp
from jax import lax
from jax.sharding import PartitionSpec as P


def local(amplitudes, pno_coef, ladder_ints, coulomb_ints, pno_energy, link_owner, link_local):
    groups = lax.axis_size("pairs")
    pair_dev = amplitudes.shape[0]
    own_rows = coulomb_ints.shape[0]
    slot_count = link_owner.shape[0]
    per_slice = slot_count // pair_dev
    capacity = max(2, (5 * slot_count + 4 * groups - 1) // (4 * groups))
    pno_width = amplitudes.shape[1]
    pao_width = pno_coef.shape[1]
    owner_group = link_owner[:, 0]
    local_index = link_local[:, 0]
    slot_order = jnp.arange(slot_count, dtype=jnp.int32)
    same_owner = (owner_group[:, None] == owner_group[None, :]) & (
        slot_order[None, :] < slot_order[:, None]
    )
    slot_rank = jnp.sum(same_owner.astype(jnp.int32), axis=1)
    bucket = owner_group * capacity + slot_rank
    places = jnp.arange(groups * capacity, dtype=jnp.int32)
    match_table = (bucket[:, None] == places[None, :]).astype(jnp.int32)
    wanted = jnp.sum(match_table * (local_index[:, None] + 1), axis=0) - 1
    asked_rows = lax.all_to_all(
        wanted.reshape(groups, capacity), "pairs", split_axis=0, concat_axis=0, tiled=True
    )
    present = asked_rows >= 0
    picked = jnp.maximum(asked_rows, 0)
    nothing = jnp.zeros((), jnp.bfloat16)
    amp_items = jnp.where(present[:, :, None, None], amplitudes[picked], nothing)
    coef_items = jnp.where(present[:, :, None, None], pno_coef[picked], nothing)
    got_amp, got_coef = (
        lax.all_to_all(amp_items, "pairs", split_axis=0, concat_axis=0, tiled=True),
        lax.all_to_all(coef_items, "pairs", split_axis=0, concat_axis=0, tiled=True),
    )
    flat_amp = got_amp.reshape(groups * capacity, pno_width, pno_width)
    flat_coef = got_coef.reshape(groups * capacity, pao_width, pno_width)
    key_rows = bucket.reshape(pair_dev, per_slice)

    def pair_terms(inputs):
        coef_p, amp_p, key_row = inputs
        coef_q = flat_coef[key_row]
        amp_q = flat_amp[key_row]
        intersection = jnp.einsum(
            "ac,lad->lcd", coef_p, coef_q, preferred_element_type=jnp.float32
        ).astype(jnp.bfloat16)
        halfway = jnp.einsum(
            "lcd,lde->lce", intersection, amp_q, preferred_element_type=jnp.float32
        ).astype(jnp.bfloat16)
        total = jnp.einsum("lce,lfe->cf", halfway, intersection, preferred_element_type=jnp.float32)
        ladder_half = jnp.einsum(
            "qcd,de->qce", ladder_ints, amp_p, preferred_element_type=jnp.float32
        ).astype(jnp.bfloat16)
        total = total + jnp.einsum(
            "qce,qfe->cf", ladder_half, ladder_ints, preferred_element_type=jnp.float32
        )
        return total

    partial_value = lax.map(pair_terms, (pno_coef, amplitudes, key_rows))
    first_row = lax.axis_index("aux") * own_rows
    amp_mine = lax.dynamic_slice_in_dim(amplitudes, first_row, own_rows, 0)
    summed = lax.psum(partial_value, "aux")
    reduced = lax.dynamic_slice_in_dim(summed, first_row, own_rows, 0)
    residual = coulomb_ints.astype(jnp.float32) + reduced
    denominator = pno_energy[:, :, None] + pno_energy[:, None, :]
    return amp_mine.astype(jnp.float32) - residual / denominator


def solution(mesh):
    in_specs = (
        P("pairs", None, None),
        P("pairs", None, None),
        P("aux", None, None),
        P(("pairs", "aux"), None, None),
        P(("pairs", "aux"), None),
        P(("pairs", "aux"), None),
        P(("pairs", "aux"), None),
    )
    out_specs = P(("pairs", "aux"), None, None)
    return jax.shard_map(local, mesh=mesh, in_specs=in_specs, out_specs=out_specs, check_vma=False)
```

profile of v0, /device:TPU:2, one launch (start us, length us, event | category | flops | bytes accessed | tf_op | source)
XLA Modules:
  0.0 579.0 jit_solution(16118599690050762865)
XLA Ops:
  9.0 19.1 %all_to_all.16 = s32[64,1,2]{2,1,0:T(1,128)S(1)} all-to-all(s32[64,1,2]{2,1,0:T(1,128)S(1)} %bitcast.97), channel_id=1, replica_groups=mesh['pairs'=64,'aux'=8] {'pairs'}, dimensions={0} | all-to-all | bytes 1024 | tf_op jit(solution)/shard_map/all_to_all | solution.py:27
  28.6 4.1 gather_fusion.3
  32.7 4.5 broadcast_select_fusion.1
  37.2 6.6 %all-to-all-start.2 = ((bf16[64,2,128,128]{3,2,1,0:T(8,128)(2,1)}), bf16[64,2,128,128]{3,2,1,0:T(8,128)(2,1)}, u32[]{:S(2)}, u32[]{:S(2)}) async-start(bf16[64,2,128,128]{3,2,1,0:T(8,128)(2,1)} %broadcast_select_fusion.1), calls=%async_computation.2 | async-start | bytes 8388608 | tf_op jit(solution)/shard_map/all_to_all | solution.py:36
  43.8 6.6 %gather_fusion.2 = bf16[128,256,128]{2,1,0:T(8,128)(2,1)} fusion(bf16[16,256,128]{2,1,0:T(8,128)(2,1)S(1)} %copy-done.1, s32[1024]{0:T(1024)S(1)} %pad_clamp_fusion.1), kind=kCustom, calls=%fused_computation.2 | custom fusion | bytes 16777728 | tf_op jit(solution)/shard_map/gather | solution.py:34
  50.4 7.2 %broadcast_select_fusion = bf16[64,2,256,128]{3,2,1,0:T(8,128)(2,1)} fusion(bf16[64,2,256,128]{3,2,1,0:T(8,128)(2,1)} %bitcast.95, pred[64,2]{1,0:T(8,128)(4,1)S(1)} %copy.33), kind=kLoop, calls=%fused_computation.27 | loop fusion | flops 4194304 | bytes 16777344 | tf_op jit(solution)/shard_map/jit(_where)/select_n | solution.py:34
  57.6 81.1 %all-to-all-done.2 = bf16[64,2,128,128]{3,2,1,0:T(8,128)(2,1)} async-done(((bf16[64,2,128,128]{3,2,1,0:T(8,128)(2,1)}), bf16[64,2,128,128]{3,2,1,0:T(8,128)(2,1)}, u32[]{:S(2)}, u32[]{:S(2)}) %all-to-all-start.2) | async-done | bytes 4194336 | tf_op jit(solution)/shard_map/all_to_all | solution.py:36
  138.7 7.0 %all-to-all-start.1 = ((bf16[64,2,256,128]{3,2,1,0:T(8,128)(2,1)}), bf16[64,2,256,128]{3,2,1,0:T(8,128)(2,1)}, u32[]{:S(2)}, u32[]{:S(2)}) async-start(bf16[64,2,256,128]{3,2,1,0:T(8,128)(2,1)} %broadcast_select_fusion), calls=%async_computation.1 | async-start | bytes 16777216 | tf_op jit(solution)/shard_map/all_to_all | solution.py:37
  145.9 184.1 %all-to-all-done.1 = bf16[64,2,256,128]{3,2,1,0:T(8,128)(2,1)} async-done(((bf16[64,2,256,128]{3,2,1,0:T(8,128)(2,1)}), bf16[64,2,256,128]{3,2,1,0:T(8,128)(2,1)}, u32[]{:S(2)}, u32[]{:S(2)}) %all-to-all-start.1) | async-done | bytes 8388640 | tf_op jit(solution)/shard_map/all_to_all | solution.py:37
  330.0 156.9 %while.10 = (s32[]{:T(128)}, f32[16,128,128]{2,1,0:T(8,128)}, s32[16,6]{1,0:T(8,128)S(1)}, bf16[128,256,128]{2,1,0:T(8,128)(2,1)}, bf16[16,256,128]{2,1,0:T(8,12...) while((s32[]{:T(128)}, f32[16,128,128]{2,1,0:T(8,128)}, ...), condition=%wide.region_3.4_spmd, body=%wide.region_2.3_spmd.sunk | while | flops 437076992 | bytes 5084381 | solution.py:62
  330.0 4.0 gather_fusion
  334.4 2.8 gather_fusion.1
  337.6 2.3 fusion.48
  339.9 4.0 gather_fusion
  344.2 2.8 gather_fusion.1
  349.7 4.0 gather_fusion
  354.0 2.8 gather_fusion.1
  359.5 4.0 gather_fusion
  363.8 2.8 gather_fusion.1
  369.3 4.0 gather_fusion
  373.6 2.8 gather_fusion.1
  379.1 4.0 gather_fusion
  383.4 2.8 gather_fusion.1
  388.9 4.0 gather_fusion
  393.2 2.8 gather_fusion.1
  396.4 2.3 fusion.48
  398.7 4.0 gather_fusion
  403.0 2.8 gather_fusion.1
  408.5 4.0 gather_fusion
  412.8 2.8 gather_fusion.1
  418.3 4.0 gather_fusion
  422.6 2.8 gather_fusion.1
  425.8 2.3 fusion.48
  428.1 4.0 gather_fusion
  432.4 2.8 gather_fusion.1
  437.9 4.0 gather_fusion
  442.2 2.8 gather_fusion.1
  445.4 2.3 fusion.48
  447.7 4.0 gather_fusion
  452.0 2.8 gather_fusion.1
  455.2 2.3 fusion.48
  457.5 4.0 gather_fusion
  461.8 2.8 gather_fusion.1
  467.3 4.0 gather_fusion
  471.6 2.8 gather_fusion.1
  477.1 4.0 gather_fusion
  481.4 2.8 gather_fusion.1
  486.9 83.6 %all-reduce.2.cloned.1.call-done = f32[16,128,128]{2,1,0:T(8,128)} async-done(((f32[16,128,128]{2,1,0:T(8,128)}), f32[16,128,128]{2,1,0:T(8,128)}) %all-reduce.2.cloned.1.call-update) | async-done | bytes 1048592 | tf_op jit(solution)/shard_map/psum | solution.py:65
  (102 shorter events, 41.5 us)
Async XLA Ops:
  37.2 6.6 %copy-start.1 = (bf16[16,256,128]{2,1,0:T(8,128)(2,1)S(1)}, bf16[16,256,128]{2,1,0:T(8,128)(2,1)}, u32[]{:S(2)}) copy-start(bf16[16,256,128]{2,1,0:T(8,128)(2,1)} %param.10) | copy-start | bytes 3145732
  37.2 101.5 %all-to-all-start.2 = ((bf16[64,2,128,128]{3,2,1,0:T(8,128)(2,1)}), bf16[64,2,128,128]{3,2,1,0:T(8,128)(2,1)}, u32[]{:S(2)}, u32[]{:S(2)}) async-start(bf16[64,2,128,128]{3,2,1,0:T(8,128)(2,1)} %broadcast_select_fusion.1), calls=%async_computation.2 | async-start | bytes 8388608 | tf_op jit(solution)/shard_map/all_to_all | solution.py:36
  57.6 272.4 %copy-start = (bf16[40,128,128]{2,1,0:T(8,128)(2,1)S(1)}, bf16[40,128,128]{2,1,0:T(8,128)(2,1)}, u32[]{:S(2)}) copy-start(bf16[40,128,128]{2,1,0:T(8,128)(2,1)} %param.11) | copy-start | bytes 3932164
  138.7 191.3 %all-to-all-start.1 = ((bf16[64,2,256,128]{3,2,1,0:T(8,128)(2,1)}), bf16[64,2,256,128]{3,2,1,0:T(8,128)(2,1)}, u32[]{:S(2)}, u32[]{:S(2)}) async-start(bf16[64,2,256,128]{3,2,1,0:T(8,128)(2,1)} %broadcast_select_fusion), calls=%async_computation.1 | async-start | bytes 16777216 | tf_op jit(solution)/shard_map/all_to_all | solution.py:37
  145.6 424.8 %all-reduce.2.cloned.1.call-start = ((), (), s32[]{:S(2)}) async-start(), calls=%async_computation.3 | async-start | bytes 2097152 | tf_op jit(solution)/shard_map/psum | solution.py:65
  330.0 240.5 %copy-start.2 = (bf16[2,128,128]{2,1,0:T(8,128)(2,1)S(1)}, bf16[2,128,128]{2,1,0:T(8,128)(2,1)}, u32[]{:S(2)}) copy-start(bf16[2,128,128]{2,1,0:T(8,128)(2,1)} %param.12) | copy-start | bytes 196612
  330.0 240.5 %copy-start.3 = (f32[2,128]{1,0:T(2,128)S(1)}, f32[2,128]{1,0:T(2,128)}, u32[]{:S(2)}) copy-start(f32[2,128]{1,0:T(2,128)} %param.13) | copy-start | bytes 3076
Sparse Core Ops, SparseCore 0:
  487.0 83.4 all-reduce.1
where the time goes:
time: 582 us; the launch traced here: 579 us
  waiting for transfers between devices  349 us (60%)
  local copies, waits for them, and re-layouts  120 us (21%)
  matrix products  47.7 us (8%)
  blocking collectives  19.1 us (3%)
  other arithmetic  16.2 us (3%)
  starting transfers between devices  13.6 us (2%)
  between operations  13.5 us (2%)
    all_to_all x1, waiting for transfers between devices, local(): lax.all_to_all(coef_items, 'pairs', split_axis=0, concat_axis=0, tiled=True)  184 us
    psum x1, waiting for transfers between devices, local(): summed = lax.psum(partial_value, 'aux')  83.6 us
    all_to_all x1, waiting for transfers between devices, local(): lax.all_to_all(amp_items, 'pairs', split_axis=0, concat_axis=0, tiled=True)  81.1 us
    gather x16, local copies, waits for them, and re-layouts, pair_terms(): coef_q = flat_coef[key_row]  64 us
    gather x16, local copies, waits for them, and re-layouts, pair_terms(): amp_q = flat_amp[key_row]  44.3 us
    dot_general x16, matrix products, pair_terms(): jnp.einsum('qce,qfe->cf', ladder_half, ladder_ints, preferred_element_typ...  36.2 us
    all_to_all x1, blocking collectives, local(): lax.all_to_all(wanted.reshape(groups, capacity), 'pairs', split_axis=0, c...  19.1 us
  transfers between devices with their start and end apart: 3, of which 3 were waited for; matrix products, arithmetic and copies ran while one was open for 2% of the time, Pallas kernels for 0%

commit v1 on v0

--- a/solution.py
+++ b/solution.py
@@ -1,7 +1,15 @@
+import functools
 import jax
 import jax.numpy as jnp
 from jax import lax
 from jax.sharding import PartitionSpec as P
+
+
+def post_the_ports(content, chip_axis):
+    return lax.all_gather(content, chip_axis).sum(axis=0)
+
+
+divide_the_yards = functools.partial(post_the_ports, chip_axis="aux")
 
 
 def local(amplitudes, pno_coef, ladder_ints, coulomb_ints, pno_energy, link_owner, link_local):
@@ -62,7 +70,7 @@
     partial_value = lax.map(pair_terms, (pno_coef, amplitudes, key_rows))
     first_row = lax.axis_index("aux") * own_rows
     amp_mine = lax.dynamic_slice_in_dim(amplitudes, first_row, own_rows, 0)
-    summed = lax.psum(partial_value, "aux")
+    summed = divide_the_yards(partial_value)
     reduced = lax.dynamic_slice_in_dim(summed, first_row, own_rows, 0)
     residual = coulomb_ints.astype(jnp.float32) + reduced
     denominator = pno_energy[:, :, None] + pno_energy[:, None, :]

time: 582 us -> 602 us (1.034)
  the two profiles are of different devices: /device:TPU:2 before, /device:TPU:1 now
where the time goes in v1:
time: 602 us; the launch traced here: 599 us
  waiting for transfers between devices  365 us (61%)
  local copies, waits for them, and re-layouts  120 us (20%)
  matrix products  47.7 us (8%)
  blocking collectives  20.7 us (3%)
  other arithmetic  20.3 us (3%)
  between operations  13.5 us (2%)
  starting transfers between devices  11.9 us (2%)
    all_to_all x1, waiting for transfers between devices, local(): lax.all_to_all(coef_items, 'pairs', split_axis=0, concat_axis=0, tiled=True)  186 us
    all_gather x1, waiting for transfers between devices, post_the_ports(): return lax.all_gather(content, chip_axis).sum(axis=0)  97.5 us
    all_to_all x1, waiting for transfers between devices, local(): lax.all_to_all(amp_items, 'pairs', split_axis=0, concat_axis=0, tiled=True)  82.1 us
    gather x16, local copies, waits for them, and re-layouts, pair_terms(): coef_q = flat_coef[key_row]  64 us
    gather x16, local copies, waits for them, and re-layouts, pair_terms(): amp_q = flat_amp[key_row]  44.3 us
    dot_general x16, matrix products, pair_terms(): jnp.einsum('qce,qfe->cf', ladder_half, ladder_ints, preferred_element_typ...  36.2 us
    all_to_all x1, blocking collectives, local(): lax.all_to_all(wanted.reshape(groups, capacity), 'pairs', split_axis=0, c...  20.7 us
  transfers between devices with their start and end apart: 3, of which 3 were waited for; matrix products, arithmetic and copies ran while one was open for 2% of the time, Pallas kernels for 0%

profile of v1, /device:TPU:1, one launch (start us, length us, event | category | flops | bytes accessed | tf_op | source)
XLA Modules:
  0.0 599.4 jit_solution(631277813605695512)
XLA Ops:
  9.0 20.7 %all_to_all.16 = s32[64,1,2]{2,1,0:T(1,128)S(1)} all-to-all(s32[64,1,2]{2,1,0:T(1,128)S(1)} %bitcast.99), channel_id=1, replica_groups=mesh['pairs'=64,'aux'=8] {'pairs'}, dimensions={0} | all-to-all | bytes 1024 | tf_op jit(solution)/shard_map/all_to_all | solution.py:35
  30.3 4.1 gather_fusion.3
  34.3 4.5 broadcast_select_fusion.1
  38.8 5.8 all-to-all-start.2
  44.7 6.6 %gather_fusion.2 = bf16[128,256,128]{2,1,0:T(8,128)(2,1)} fusion(bf16[16,256,128]{2,1,0:T(8,128)(2,1)S(1)} %copy-done.1, s32[1024]{0:T(1024)S(1)} %pad_clamp_fusion.1), kind=kCustom, calls=%fused_computation.2 | custom fusion | bytes 16777728 | tf_op jit(solution)/shard_map/gather | solution.py:42
  51.2 7.2 %broadcast_select_fusion = bf16[64,2,256,128]{3,2,1,0:T(8,128)(2,1)} fusion(bf16[64,2,256,128]{3,2,1,0:T(8,128)(2,1)} %bitcast.96, pred[64,2]{1,0:T(8,128)(4,1)S(1)} %copy.33), kind=kLoop, calls=%fused_computation.27 | loop fusion | flops 4194304 | bytes 16777344 | tf_op jit(solution)/shard_map/jit(_where)/select_n | solution.py:42
  58.5 82.1 %all-to-all-done.2 = bf16[64,2,128,128]{3,2,1,0:T(8,128)(2,1)} async-done(((bf16[64,2,128,128]{3,2,1,0:T(8,128)(2,1)}), bf16[64,2,128,128]{3,2,1,0:T(8,128)(2,1)}, u32[]{:S(2)}, u32[]{:S(2)}) %all-to-all-start.2) | async-done | bytes 4194336 | tf_op jit(solution)/shard_map/all_to_all | solution.py:44
  140.6 6.0 %all-to-all-start.1 = ((bf16[64,2,256,128]{3,2,1,0:T(8,128)(2,1)}), bf16[64,2,256,128]{3,2,1,0:T(8,128)(2,1)}, u32[]{:S(2)}, u32[]{:S(2)}) async-start(bf16[64,2,256,128]{3,2,1,0:T(8,128)(2,1)} %broadcast_select_fusion), calls=%async_computation.1 | async-start | bytes 16777216 | tf_op jit(solution)/shard_map/all_to_all | solution.py:45
  146.8 185.5 %all-to-all-done.1 = bf16[64,2,256,128]{3,2,1,0:T(8,128)(2,1)} async-done(((bf16[64,2,256,128]{3,2,1,0:T(8,128)(2,1)}), bf16[64,2,256,128]{3,2,1,0:T(8,128)(2,1)}, u32[]{:S(2)}, u32[]{:S(2)}) %all-to-all-start.1) | async-done | bytes 8388640 | tf_op jit(solution)/shard_map/all_to_all | solution.py:45
  332.4 156.8 %while.10 = (s32[]{:T(128)}, f32[16,128,128]{2,1,0:T(8,128)}, s32[16,6]{1,0:T(8,128)S(1)}, bf16[128,256,128]{2,1,0:T(8,128)(2,1)}, bf16[16,256,128]{2,1,0:T(8,12...) while((s32[]{:T(128)}, f32[16,128,128]{2,1,0:T(8,128)}, ...), condition=%wide.region_3.4_spmd, body=%wide.region_2.3_spmd.sunk | while | flops 437076992 | bytes 5084381 | solution.py:70
  332.4 4.0 gather_fusion
  336.7 2.8 gather_fusion.1
  339.9 2.3 fusion.48
  342.2 4.0 gather_fusion
  346.6 2.8 gather_fusion.1
  352.0 4.0 gather_fusion
  356.3 2.8 gather_fusion.1
  361.8 4.0 gather_fusion
  366.1 2.8 gather_fusion.1
  371.6 4.0 gather_fusion
  375.9 2.8 gather_fusion.1
  381.4 4.0 gather_fusion
  385.7 2.8 gather_fusion.1
  391.2 4.0 gather_fusion
  395.5 2.8 gather_fusion.1
  398.7 2.3 fusion.48
  401.0 4.0 gather_fusion
  405.3 2.8 gather_fusion.1
  410.8 4.0 gather_fusion
  415.1 2.8 gather_fusion.1
  420.6 4.0 gather_fusion
  424.9 2.8 gather_fusion.1
  428.1 2.3 fusion.48
  430.4 4.0 gather_fusion
  434.7 2.8 gather_fusion.1
  440.2 4.0 gather_fusion
  444.5 2.8 gather_fusion.1
  447.7 2.3 fusion.48
  450.0 4.0 gather_fusion
  454.3 2.8 gather_fusion.1
  459.8 4.0 gather_fusion
  464.1 2.8 gather_fusion.1
  469.6 4.0 gather_fusion
  474.0 2.8 gather_fusion.1
  479.4 4.0 gather_fusion
  483.8 2.8 gather_fusion.1
  489.2 97.5 %all-gather.3.cloned.1.call-done = f32[128,128,128]{2,1,0:T(8,128)} async-done(((f32[16,128,128]{2,1,0:T(8,128)}), f32[128,128,128]{2,1,0:T(8,128)}) %all-gather.3.cloned.1.call-update) | async-done | bytes 8388624 | tf_op jit(solution)/shard_map/all_gather | solution.py:9
  586.7 4.2 reduce_sum.35
  (103 shorter events, 43.7 us)
Async XLA Ops:
  38.8 5.8 copy-start.1
  38.8 101.8 %all-to-all-start.2 = ((bf16[64,2,128,128]{3,2,1,0:T(8,128)(2,1)}), bf16[64,2,128,128]{3,2,1,0:T(8,128)(2,1)}, u32[]{:S(2)}, u32[]{:S(2)}) async-start(bf16[64,2,128,128]{3,2,1,0:T(8,128)(2,1)} %broadcast_select_fusion.1), calls=%async_computation.2 | async-start | bytes 8388608 | tf_op jit(solution)/shard_map/all_to_all | solution.py:44
  58.5 273.9 %copy-start = (bf16[40,128,128]{2,1,0:T(8,128)(2,1)S(1)}, bf16[40,128,128]{2,1,0:T(8,128)(2,1)}, u32[]{:S(2)}) copy-start(bf16[40,128,128]{2,1,0:T(8,128)(2,1)} %param.11) | copy-start | bytes 3932164
  140.6 191.8 %all-to-all-start.1 = ((bf16[64,2,256,128]{3,2,1,0:T(8,128)(2,1)}), bf16[64,2,256,128]{3,2,1,0:T(8,128)(2,1)}, u32[]{:S(2)}, u32[]{:S(2)}) async-start(bf16[64,2,256,128]{3,2,1,0:T(8,128)(2,1)} %broadcast_select_fusion), calls=%async_computation.1 | async-start | bytes 16777216 | tf_op jit(solution)/shard_map/all_to_all | solution.py:45
  146.6 440.1 %all-gather.3.cloned.1.call-start = ((), (), s32[]{:S(2)}) async-start(), calls=%async_computation.3 | async-start | bytes 9437184 | tf_op jit(solution)/shard_map/all_gather | solution.py:9
  586.7 4.2 copy-start.2
  586.7 4.2 copy-start.3
Sparse Core Ops, SparseCore 0:
  489.4 97.3 all-gather.2
